TPU v7x, 32 devices: a whole 2x2x4 slice. The times are simulated.
32 devices in a mesh: dp: 8 (over z, core), mp: 4 (over y, x).
Axes of the slice: x: 2, y: 2, z: 4, core: 2. Of those that a mesh axis runs over, the one named last changes fastest.
Arguments:
- tokens: bfloat16 [16, 640, 2048], P('dp', 'mp'), may hold values from -6 to 6
- lengths: int32 [16], P('dp'), may hold values from 320 to 640, as said below
- w_query: bfloat16 [2048, 2048], P(None, 'mp'), may hold values from -0.125 to 0.125
- w_key: bfloat16 [2048, 2048], P(None, 'mp'), may hold values from -0.125 to 0.125
- w_value: bfloat16 [2048, 2048], P(None, 'mp'), may hold values from -0.125 to 0.125
- b_query: float32 [16, 128], P('mp'), may hold values from -3 to 3
- b_value: float32 [16, 128], P('mp'), may hold values from -2 to 2
- w_out: bfloat16 [2048, 2048], P('mp'), may hold values from -1 to 1
- b_out: float32 [2048], replicated, may hold values from -2 to 2
- w_up: bfloat16 [2048, 8192], P(None, 'mp'), may hold values from -0.125 to 0.125
- b_up: float32 [64, 128], P('mp'), may hold values from -2 to 2
- w_down: bfloat16 [8192, 2048], P('mp'), may hold values from -0.0625 to 0.0625
- b_down: float32 [2048], replicated, may hold values from -2 to 2
- norm1_gain: float32 [2048], replicated, may hold values from 0.5 to 1.5
- norm1_shift: float32 [2048], replicated, may hold values from -1.5 to 1.5
- norm2_gain: float32 [2048], replicated, may hold values from 0.5 to 1.5
- norm2_shift: float32 [2048], replicated, may hold values from -1.5 to 1.5
- cotangent: bfloat16 [16, 640, 2048], P('dp', 'mp'), may hold values from -6 to 6
Outputs:
- output: bfloat16 [16, 640, 2048], P('dp', 'mp')
- grad_tokens: bfloat16 [16, 640, 2048], P('dp', 'mp')
- grad_w_query: float32 [2048, 2048], P('dp', 'mp')
- grad_w_key: float32 [2048, 2048], P('dp', 'mp')
- grad_w_value: float32 [2048, 2048], P('dp', 'mp')
- grad_b_query: float32 [16, 128], P('mp', 'dp')
- grad_b_value: float32 [16, 128], P('mp', 'dp')
- grad_w_out: float32 [2048, 2048], P('mp', 'dp')
- grad_b_out: float32 [2048], P(('dp', 'mp'))
- grad_w_up: float32 [2048, 8192], P('dp', 'mp')
- grad_b_up: float32 [64, 128], P('mp', 'dp')
- grad_w_down: float32 [8192, 2048], P('mp', 'dp')
- grad_b_down: float32 [2048], P(('dp', 'mp'))
- grad_norm1_gain: float32 [2048], P(('dp', 'mp'))
- grad_norm1_shift: float32 [2048], P(('dp', 'mp'))
- grad_norm2_gain: float32 [2048], P(('dp', 'mp'))
- grad_norm2_shift: float32 [2048], P(('dp', 'mp'))
Inputs may be any that keep to these rules, and one draw needn't show every extreme that they name: `lengths`: each item has 320 to 640 valid slots, the first ones; some item is full.
All inputs are finite; a program needn't handle non-finite values.
Results may differ from a plain program's by a relative error of at most 0.02.
Values may be sent and summed in bfloat16 or wider, within the bound.
No kernel may reach another device: no remote copies, remote signals or barrier semaphores. Data moves between devices by JAX's collectives and lax.ppermute only.
A program may use at most 256 MiB of HBM per device.

v0:
```python
from functools import partial
import jax
import jax.numpy as jnp
from jax import lax
from jax.sharding import PartitionSpec as P

HEAD_DIM = 128


def layer_norm(values, gain, shift):
    centre = values - jnp.mean(values, axis=-1, keepdims=True)
    spread = jnp.mean(centre * centre, axis=-1, keepdims=True)
    return centre * lax.rsqrt(spread + 1e-05) * gain + shift


def allowed_keys(lengths, seq_len):
    places = jnp.arange(seq_len)
    causal = places[None, :] <= places[:, None]
    inside = places[None, None, :] < lengths[:, None, None]
    return (causal[None] & inside)[:, None]


def head_scores(query_heads, key_heads, allowed):
    scores = jnp.einsum(
        "iqhd,ikhd->ihqk", query_heads, key_heads, preferred_element_type=jnp.float32
    ) * HEAD_DIM ** (-0.5)
    return jnp.where(allowed, scores, -1e30)


def body(
    tokens,
    lengths,
    w_query,
    w_key,
    w_value,
    b_query,
    b_value,
    w_out,
    b_out,
    w_up,
    b_up,
    w_down,
    b_down,
    norm1_gain,
    norm1_shift,
    norm2_gain,
    norm2_shift,
    cotangent,
):
    f32 = jnp.float32
    bf16 = jnp.bfloat16
    rows_in = tokens.astype(f32)
    normed_one = layer_norm(rows_in, norm1_gain, norm1_shift).astype(bf16)
    full_one = lax.all_gather(normed_one, "mp", axis=1, tiled=True)
    items, seq_len = (full_one.shape[0], full_one.shape[1])
    heads_here = w_query.shape[1] // HEAD_DIM
    split = (items, seq_len, heads_here, HEAD_DIM)

    def project(weight):
        return jnp.einsum("isd,de->ise", full_one, weight, preferred_element_type=f32)

    queries = (project(w_query) + b_query.reshape(-1)).astype(bf16)
    keys_all = project(w_key).astype(bf16)
    values_all = (project(w_value) + b_value.reshape(-1)).astype(bf16)
    query_heads = queries.reshape(split)
    key_heads = keys_all.reshape(split)
    value_heads = values_all.reshape(split)
    allowed = allowed_keys(lengths, seq_len)
    scores = head_scores(query_heads, key_heads, allowed)
    row_max = jnp.max(scores, axis=-1, keepdims=True)
    raw_weights = jnp.exp(scores - row_max)
    row_total = jnp.sum(raw_weights, axis=-1, keepdims=True)
    probs = (raw_weights / row_total).astype(bf16)
    mixed = (
        jnp.einsum("ihqk,ikhd->iqhd", probs, value_heads, preferred_element_type=f32)
        .reshape(items, seq_len, -1)
        .astype(bf16)
    )
    attn_terms = jnp.einsum("ise,ed->isd", mixed, w_out, preferred_element_type=f32)
    attn_rows = lax.psum_scatter(
        attn_terms.astype(jnp.bfloat16), "mp", scatter_dimension=1, tiled=True
    ).astype(jnp.float32)
    middle = rows_in + attn_rows + b_out
    normed_two = layer_norm(middle, norm2_gain, norm2_shift).astype(bf16)
    full_two = lax.all_gather(normed_two, "mp", axis=1, tiled=True)
    hidden_pre = jnp.einsum(
        "isd,df->isf", full_two, w_up, preferred_element_type=f32
    ) + b_up.reshape(-1)
    hidden = jax.nn.gelu(hidden_pre, approximate=False).astype(bf16)
    ffn_terms = jnp.einsum("isf,fd->isd", hidden, w_down, preferred_element_type=f32)
    ffn_rows = lax.psum_scatter(
        ffn_terms.astype(jnp.bfloat16), "mp", scatter_dimension=1, tiled=True
    ).astype(jnp.float32)
    result = (middle + ffn_rows + b_down).astype(bf16)
    grad_out = cotangent.astype(f32)
    grad_full = lax.all_gather(cotangent, "mp", axis=1, tiled=True)
    grad_w_down = jnp.einsum("isf,isd->fd", hidden, grad_full, preferred_element_type=f32)
    grad_b_down = jnp.sum(grad_out, axis=(0, 1))
    grad_hidden = jnp.einsum("isd,fd->isf", grad_full, w_down, preferred_element_type=f32)
    _, gelu_back = jax.vjp(partial(jax.nn.gelu, approximate=False), hidden_pre)
    grad_pre = gelu_back(grad_hidden)[0].astype(bf16)
    grad_w_up = jnp.einsum("isd,isf->df", full_two, grad_pre, preferred_element_type=f32)
    grad_b_up = jnp.sum(grad_pre, axis=(0, 1), dtype=f32).reshape(b_up.shape)
    back_terms = jnp.einsum("isf,df->isd", grad_pre, w_up, preferred_element_type=f32)
    back_rows = lax.psum_scatter(
        back_terms.astype(jnp.bfloat16), "mp", scatter_dimension=1, tiled=True
    ).astype(jnp.float32)
    _, second_back = jax.vjp(layer_norm, middle, norm2_gain, norm2_shift)
    grad_mid_norm, grad_gain_two, grad_shift_two = second_back(back_rows)
    grad_middle = grad_out + grad_mid_norm
    grad_b_out = jnp.sum(grad_middle, axis=(0, 1))
    middle_full = lax.all_gather(grad_middle.astype(bf16), "mp", axis=1, tiled=True)
    grad_w_out = jnp.einsum("ise,isd->ed", mixed, middle_full, preferred_element_type=f32)
    grad_mixed = (
        jnp.einsum("isd,ed->ise", middle_full, w_out, preferred_element_type=f32)
        .astype(bf16)
        .reshape(split)
    )
    again = head_scores(query_heads, key_heads, allowed)
    probs_full = jnp.exp(again - row_max) / row_total
    probs_low = probs_full.astype(bf16)
    grad_value = (
        jnp.einsum("ihqk,iqhd->ikhd", probs_low, grad_mixed, preferred_element_type=f32)
        .astype(bf16)
        .reshape(items, seq_len, -1)
    )
    grad_probs = jnp.einsum("iqhd,ikhd->ihqk", grad_mixed, value_heads, preferred_element_type=f32)
    inner = jnp.sum(probs_full * grad_probs, axis=-1, keepdims=True)
    grad_scores = (probs_full * (grad_probs - inner)).astype(bf16)
    grad_query = (
        (
            jnp.einsum("ihqk,ikhd->iqhd", grad_scores, key_heads, preferred_element_type=f32)
            * HEAD_DIM ** (-0.5)
        )
        .astype(bf16)
        .reshape(items, seq_len, -1)
    )
    grad_key = (
        (
            jnp.einsum("ihqk,iqhd->ikhd", grad_scores, query_heads, preferred_element_type=f32)
            * HEAD_DIM ** (-0.5)
        )
        .astype(bf16)
        .reshape(items, seq_len, -1)
    )

    def weight_grad(grad_cols):
        return jnp.einsum("isd,ise->de", full_one, grad_cols, preferred_element_type=f32)

    grad_w_query = weight_grad(grad_query)
    grad_w_key = weight_grad(grad_key)
    grad_w_value = weight_grad(grad_value)
    grad_b_query = jnp.sum(grad_query, axis=(0, 1), dtype=f32).reshape(b_query.shape)
    grad_b_value = jnp.sum(grad_value, axis=(0, 1), dtype=f32).reshape(b_value.shape)
    back_one = (
        jnp.einsum("ise,de->isd", grad_query, w_query, preferred_element_type=f32)
        + jnp.einsum("ise,de->isd", grad_key, w_key, preferred_element_type=f32)
        + jnp.einsum("ise,de->isd", grad_value, w_value, preferred_element_type=f32)
    )
    rows_one = lax.psum_scatter(
        back_one.astype(jnp.bfloat16), "mp", scatter_dimension=1, tiled=True
    ).astype(jnp.float32)
    _, first_back = jax.vjp(layer_norm, rows_in, norm1_gain, norm1_shift)
    grad_in_norm, grad_gain_one, grad_shift_one = first_back(rows_one)
    grad_inputs = (grad_middle + grad_in_norm).astype(bf16)
    every_sum = (
        lax.psum_scatter(
            grad_w_query.astype(jnp.bfloat16), "dp", scatter_dimension=0, tiled=True
        ).astype(jnp.float32),
        lax.psum_scatter(
            grad_w_key.astype(jnp.bfloat16), "dp", scatter_dimension=0, tiled=True
        ).astype(jnp.float32),
        lax.psum_scatter(
            grad_w_value.astype(jnp.bfloat16), "dp", scatter_dimension=0, tiled=True
        ).astype(jnp.float32),
        lax.psum_scatter(
            grad_b_query.astype(jnp.bfloat16), "dp", scatter_dimension=1, tiled=True
        ).astype(jnp.float32),
        lax.psum_scatter(
            grad_b_value.astype(jnp.bfloat16), "dp", scatter_dimension=1, tiled=True
        ).astype(jnp.float32),
        lax.psum_scatter(
            grad_w_out.astype(jnp.bfloat16), "dp", scatter_dimension=1, tiled=True
        ).astype(jnp.float32),
        lax.psum_scatter(
            grad_w_up.astype(jnp.bfloat16), "dp", scatter_dimension=0, tiled=True
        ).astype(jnp.float32),
        lax.psum_scatter(
            grad_w_down.astype(jnp.bfloat16), "dp", scatter_dimension=1, tiled=True
        ).astype(jnp.float32),
        lax.psum_scatter(
            grad_b_up.astype(jnp.bfloat16), "dp", scatter_dimension=1, tiled=True
        ).astype(jnp.float32),
    )
    (
        sum_w_query,
        sum_w_key,
        sum_w_value,
        sum_b_query,
        sum_b_value,
        sum_w_out,
        sum_w_up,
        sum_w_down,
        sum_b_up,
    ) = every_sum
    vector_sums = (
        lax.psum_scatter(grad_b_out, ("dp", "mp"), scatter_dimension=0, tiled=True),
        lax.psum_scatter(grad_b_down, ("dp", "mp"), scatter_dimension=0, tiled=True),
        lax.psum_scatter(grad_gain_one, ("dp", "mp"), scatter_dimension=0, tiled=True),
        lax.psum_scatter(grad_shift_one, ("dp", "mp"), scatter_dimension=0, tiled=True),
        lax.psum_scatter(grad_gain_two, ("dp", "mp"), scatter_dimension=0, tiled=True),
        lax.psum_scatter(grad_shift_two, ("dp", "mp"), scatter_dimension=0, tiled=True),
    )
    sum_b_out, sum_b_down, sum_gain_one, sum_shift_one, sum_gain_two, sum_shift_two = vector_sums
    return (
        result,
        grad_inputs,
        sum_w_query,
        sum_w_key,
        sum_w_value,
        sum_b_query,
        sum_b_value,
        sum_w_out,
        sum_b_out,
        sum_w_up,
        sum_b_up,
        sum_w_down,
        sum_b_down,
        sum_gain_one,
        sum_shift_one,
        sum_gain_two,
        sum_shift_two,
    )


def solution(mesh):
    return jax.shard_map(
        body,
        mesh=mesh,
        in_specs=(
            P("dp", "mp", None),
            P("dp"),
            P(None, "mp"),
            P(None, "mp"),
            P(None, "mp"),
            P("mp", None),
            P("mp", None),
            P("mp", None),
            P(),
            P(None, "mp"),
            P("mp", None),
            P("mp", None),
            P(),
            P(),
            P(),
            P(),
            P(),
            P("dp", "mp", None),
        ),
        out_specs=(
            P("dp", "mp", None),
            P("dp", "mp", None),
            P("dp", "mp"),
            P("dp", "mp"),
            P("dp", "mp"),
            P("mp", "dp"),
            P("mp", "dp"),
            P("mp", "dp"),
            P(("dp", "mp")),
            P("dp", "mp"),
            P("mp", "dp"),
            P("mp", "dp"),
            P(("dp", "mp")),
            P(("dp", "mp")),
            P(("dp", "mp")),
            P(("dp", "mp")),
            P(("dp", "mp")),
        ),
        check_vma=False,
    )
```

profile of v0, /device:TPU:0, one launch (start us, length us, event | category | flops | bytes accessed | tf_op | source)
XLA Modules:
  0.0 1041.9 jit_solution(1776042553797564077)
XLA Ops:
  15.3 62.6 %all-gather.5.cloned.1.call-done = bf16[2,640,2048]{2,1,0:T(8,128)(2,1)} async-done(((bf16[2,160,2048]{2,1,0:T(8,128)(2,1)}), bf16[2,640,2048]{2,1,0:T(8,128)(2,1)}) %all-gather.5.cloned.1.call-update) | async-done | bytes 5242896 | tf_op jit(solution)/shard_map/all_gather | solution.py:54
  89.4 11.4 %fusion.92 = (f32[2,4,640]{2,1,0:T(4,128)S(1)}, f32[2,4,640,640]{2,3,1,0:T(8,128)}) fusion(pred[2,640,640]{1,2,0:T(8,128)(4,1)} %broadcast_and_fusion, bf16[2,640,4,128]{1,3,2,0:T(8,128)(2,1)} %bitcast.133, bf16[2,640,4,128]{1,3,2,0:T(8,128)(2,1)} %bitcast.127), kind=kOutput, calls=%fused_computation.134 | convolution fusion | flops 851968640 | bytes 16568320 | tf_op jit(solution)/shard_map/sub | solution.py:71
  115.0 61.4 %reduce-scatter.20.cloned.1.call-done = bf16[2,160,2048]{2,1,0:T(8,128)(2,1)} async-done(((bf16[2,640,2048]{2,1,0:T(8,128)(2,1)}), bf16[2,160,2048]{2,1,0:T(8,128)(2,1)}) %reduce-scatter.20.cloned.1.call-update) | async-done | bytes 1310736 | tf_op jit(solution)/shard_map/reduce_scatter | solution.py:80
  182.0 60.4 %all-gather.7.cloned.1.call-done = bf16[2,640,2048]{2,1,0:T(8,128)(2,1)} async-done(((bf16[2,160,2048]{2,1,0:T(8,128)(2,1)}), bf16[2,640,2048]{2,1,0:T(8,128)(2,1)}) %all-gather.7.cloned.1.call-update) | async-done | bytes 5242896 | tf_op jit(solution)/shard_map/all_gather | solution.py:85
  242.5 20.1 %fusion.48 = (u8[640,2048]{1,0:T(8,128)(4,1)}, u8[640,2048]{1,0:T(8,128)(4,1)}, f32[2,640,2048]{2,1,0:T(8,128)S(1)}) fusion(f32[2048]{0:T(1024)S(1)} %bitcast.140, bf16[2,640,2048]{2,1,0:T(8,128)(2,1)} %all-gather.7.cloned.1.call-done, bf16[2048,2048]{1,0:T(8,128)(2,1)} %param.27), kind=kOutput, calls=%fused_computation.91 | convolution fusion | flops 10771496960 | bytes 26746880 | tf_op jit(solution)/shard_map/isd,df->isf/dot_general | solution.py:86
  266.4 26.6 %multiply_convert_fusion.1 = (bf16[2,640,2048]{2,1,0:T(8,128)(2,1)}, f32[2,640,2048]{2,1,0:T(8,128)}) fusion(f32[2,640,2048]{2,1,0:T(8,128)S(1)} %get-tuple-element.41, f32[2048]{0:T(1024)S(1)} %bitcast.141, u8[640,2048]{1,0:T(8,128)(4,1)} %get-tuple-element.18, u8[640,2048]{1,0:T(8,128)(4,1)} %get-tuple-element.17), kind=kLoop, calls=%fused_computation.16 | loop fusion | flops 186122240 | bytes 28844032 | tf_op jit(solution)/shard_map/convert_element_type | solution.py:89
  293.0 12.5 %all-gather.9.cloned.1.call-done = bf16[2,640,2048]{2,1,0:T(8,128)(2,1)} async-done(((bf16[2,160,2048]{2,1,0:T(8,128)(2,1)}), bf16[2,640,2048]{2,1,0:T(8,128)(2,1)}) %all-gather.9.cloned.1.call-update) | async-done | bytes 5242896 | tf_op jit(solution)/shard_map/all_gather | solution.py:96
  305.5 25.0 %fusion.93 = (bf16[2048]{0:T(1024)(128)(2,1)S(1)}, bf16[2,640,2048]{2,1,0:T(8,128)(2,1)}) fusion(f32[2,640,2048]{2,1,0:T(8,128)} %get-tuple-element.36, bf16[2,640,2048]{2,1,0:T(8,128)(2,1)} %all-gather.9.cloned.1.call-done, bf16[2048,2048]{1,0:T(8,128)(2,1)} %param.29, f32[2,640,2048]{2,1,0:T(8,128)} %copy-done.13, f32[2048]{0:T(1024)S(1)} %bitcast.142), kind=kOutput, calls=%fused_computation.135 | convolution fusion | flops 10779359232 | bytes 39858176 | tf_op jit(solution)/shard_map/isd,fd->isf/dot_general | solution.py:99
  330.5 16.6 %fusion.21 = bf16[2,640,2048]{2,1,0:T(8,128)(2,1)} fusion(bf16[2,640,2048]{2,1,0:T(8,128)(2,1)} %get-tuple-element.49, bf16[2048,2048]{1,0:T(8,128)(2,1)} %param.27), kind=kOutput, calls=%fused_computation.46 | convolution fusion | flops 10740039680 | bytes 18874368 | tf_op jit(solution)/shard_map/isf,df->isd/dot_general | solution.py:104
  347.4 61.2 %reduce-scatter.24.cloned.1.call-done = bf16[2,160,2048]{2,1,0:T(8,128)(2,1)} async-done(((bf16[2,640,2048]{2,1,0:T(8,128)(2,1)}), bf16[2,160,2048]{2,1,0:T(8,128)(2,1)}) %reduce-scatter.24.cloned.1.call-update) | async-done | bytes 1310736 | tf_op jit(solution)/shard_map/reduce_scatter | solution.py:105
  417.2 16.7 %bitcast_convert_fusion.1 = bf16[2048,2048]{1,0:T(8,128)(2,1)} fusion(bf16[2,640,2048]{2,1,0:T(8,128)(2,1)} %all-gather.7.cloned.1.call-done, bf16[2,640,2048]{2,1,0:T(8,128)(2,1)} %get-tuple-element.49), kind=kOutput, calls=%fused_computation.2 | convolution fusion | flops 10741612544 | bytes 18874368 | tf_op jit(solution)/shard_map/isd,isf->df/dot_general | solution.py:102
  434.4 16.7 %bitcast_convert_fusion = bf16[2048,2048]{1,0:T(8,128)(2,1)} fusion(bf16[2,640,2048]{2,1,0:T(8,128)(2,1)} %get-tuple-element.35, bf16[2,640,2048]{2,1,0:T(8,128)(2,1)} %all-gather.9.cloned.1.call-done), kind=kOutput, calls=%fused_computation.1 | convolution fusion | flops 10741612544 | bytes 18874368 | tf_op jit(solution)/shard_map/isf,isd->fd/dot_general | solution.py:97
  451.1 26.6 %all-gather.11.cloned.1.call-done = bf16[2,640,2048]{2,1,0:T(8,128)(2,1)} async-done(((bf16[2,160,2048]{2,1,0:T(8,128)(2,1)}), bf16[2,640,2048]{2,1,0:T(8,128)(2,1)}) %all-gather.11.cloned.1.call-update) | async-done | bytes 5242896 | tf_op jit(solution)/shard_map/all_gather | solution.py:112
  573.5 16.6 %fusion.24 = bf16[2,640,2048]{2,1,0:T(8,128)(2,1)} fusion(bf16[2,640,2048]{2,1,0:T(8,128)(2,1)} %get-tuple-element.35, bf16[2048,2048]{1,0:T(8,128)(2,1)} %param.29), kind=kOutput, calls=%fused_computation.47 | convolution fusion | flops 10740039680 | bytes 18874368 | tf_op jit(solution)/shard_map/isf,fd->isd/dot_general | solution.py:90
  603.9 87.5 %reduce-scatter.38.cloned.1.call-done = bf16[2048,256]{1,0:T(8,128)(2,1)} async-done(((bf16[2048,2048]{1,0:T(8,128)(2,1)}), bf16[2048,256]{1,0:T(8,128)(2,1)}) %reduce-scatter.38.cloned.1.call-update) | async-done | bytes 1048592 | tf_op jit(solution)/shard_map/reduce_scatter | solution.py:188
  694.1 29.0 %reduce-scatter.42.cloned.1.call-done = bf16[16,4]{1,0:T(8,128)(2,1)} async-done(((bf16[128,4]{1,0:T(8,128)(2,1)}), bf16[16,4]{1,0:T(8,128)(2,1)}) %reduce-scatter.42.cloned.1.call-update) | async-done | bytes 144
  724.4 30.1 %reduce-scatter.40.cloned.1.call-done = bf16[16,4]{1,0:T(8,128)(2,1)} async-done(((bf16[128,4]{1,0:T(8,128)(2,1)}), bf16[16,4]{1,0:T(8,128)(2,1)}) %reduce-scatter.40.cloned.1.call-update) | async-done | bytes 144
  755.9 34.9 %reduce-scatter.34.cloned.1.call-done = bf16[512,256]{1,0:T(8,128)(2,1)} async-done(((bf16[512,2048]{1,0:T(8,128)(2,1)}), bf16[512,256]{1,0:T(8,128)(2,1)}) %reduce-scatter.34.cloned.1.call-update) | async-done | bytes 262160 | tf_op jit(solution)/shard_map/reduce_scatter | solution.py:182
  792.6 35.1 %reduce-scatter.32.cloned.1.call-done = bf16[256,512]{1,0:T(8,128)(2,1)} async-done(((bf16[2048,512]{1,0:T(8,128)(2,1)}), bf16[256,512]{1,0:T(8,128)(2,1)}) %reduce-scatter.32.cloned.1.call-update) | async-done | bytes 262160 | tf_op jit(solution)/shard_map/reduce_scatter | solution.py:173
  829.5 35.1 %reduce-scatter.28.cloned.1.call-done = bf16[256,512]{1,0:T(8,128)(2,1)} async-done(((bf16[2048,512]{1,0:T(8,128)(2,1)}), bf16[256,512]{1,0:T(8,128)(2,1)}) %reduce-scatter.28.cloned.1.call-update) | async-done | bytes 262160 | tf_op jit(solution)/shard_map/reduce_scatter | solution.py:167
  866.4 35.0 %reduce-scatter.30.cloned.1.call-done = bf16[256,512]{1,0:T(8,128)(2,1)} async-done(((bf16[2048,512]{1,0:T(8,128)(2,1)}), bf16[256,512]{1,0:T(8,128)(2,1)}) %reduce-scatter.30.cloned.1.call-update) | async-done | bytes 262160 | tf_op jit(solution)/shard_map/reduce_scatter | solution.py:170
  903.2 61.0 %reduce-scatter.26.cloned.1.call-done = bf16[2,160,2048]{2,1,0:T(8,128)(2,1)} async-done(((bf16[2,640,2048]{2,1,0:T(8,128)(2,1)}), bf16[2,160,2048]{2,1,0:T(8,128)(2,1)}) %reduce-scatter.26.cloned.1.call-update) | async-done | bytes 1310736 | tf_op jit(solution)/shard_map/reduce_scatter | solution.py:160
  971.7 40.7 %all-reduce.6 = (f32[2048]{0:T(1024)S(1)}, f32[2048]{0:T(1024)S(1)}, f32[2048]{0:T(1024)S(1)}, f32[2048]{0:T(1024)S(1)}, f32[2048]{0:T(1024)S(1)}, /*index=5*/f32[2048]{0:T(1024)S(1)}) all-reduce(f32[2048]{0:T(1024)S(1)} %get-tuple-element.20, f32[2048]{0:T(1024)S(1)} %get-tuple-element.23, ...), channel_id=12, replica_groups=mesh['dp'=8,'mp'=4] {'dp','mp'}, use_global_device_ids=true, to_apply=%region_24.25.clone | all-reduce | flops 12288 | bytes 98304
  1015.9 13.4 %reduce-scatter.22.cloned.1.call-done = bf16[2,160,2048]{2,1,0:T(8,128)(2,1)} async-done(((bf16[2,640,2048]{2,1,0:T(8,128)(2,1)}), bf16[2,160,2048]{2,1,0:T(8,128)(2,1)}) %reduce-scatter.22.cloned.1.call-update) | async-done | bytes 1310736 | tf_op jit(solution)/shard_map/reduce_scatter | solution.py:91
  (208 shorter events, 190.7 us)
Async XLA Ops:
  7.2 70.6 %all-gather.5.cloned.1.call-start = ((), (), s32[]{:S(2)}) async-start(), calls=%async_computation.13 | async-start | bytes 6553600 | tf_op jit(solution)/shard_map/all_gather | solution.py:54
  13.7 162.7 %reduce-scatter.20.cloned.1.call-start = ((), (), s32[]{:S(2)}) async-start(), calls=%async_computation.14 | async-start | bytes 6553600 | tf_op jit(solution)/shard_map/reduce_scatter | solution.py:80
  114.9 127.6 %all-gather.7.cloned.1.call-start = ((), (), s32[]{:S(2)}) async-start(), calls=%async_computation.15 | async-start | bytes 6553600 | tf_op jit(solution)/shard_map/all_gather | solution.py:85
  178.3 235.0 %copy-start.24 = (f32[2,160]{1,0:T(2,128)}, f32[2,160]{1,0:T(2,128)S(1)}, u32[]{:S(2)}) copy-start(f32[2,160]{1,0:T(2,128)S(1)} %broadcast_multiply_fusion) | copy-start | bytes 3844
  179.1 234.3 %copy-start.28 = (f32[2,160]{1,0:T(2,128)}, f32[2,160]{1,0:T(2,128)S(1)}, u32[]{:S(2)}) copy-start(f32[2,160]{1,0:T(2,128)S(1)} %fusion.86) | copy-start | bytes 3844
  181.0 124.5 %all-gather.9.cloned.1.call-start = ((), (), s32[]{:S(2)}) async-start(), calls=%async_computation.17 | async-start | bytes 6553600 | tf_op jit(solution)/shard_map/all_gather | solution.py:96
  181.6 227.0 %reduce-scatter.24.cloned.1.call-start = ((), (), s32[]{:S(2)}) async-start(), calls=%async_computation.18 | async-start | bytes 6553600 | tf_op jit(solution)/shard_map/reduce_scatter | solution.py:105
  347.1 130.6 %all-gather.11.cloned.1.call-start = ((), (), s32[]{:S(2)}) async-start(), calls=%async_computation.19 | async-start | bytes 6553600 | tf_op jit(solution)/shard_map/all_gather | solution.py:112
  416.3 173.9 %reduce-scatter.44.cloned.1.call-start = ((), (), s32[]{:S(2)}) async-start(), calls=%async_computation.29 | async-start | bytes 36864
  417.1 184.0 %reduce-scatter.36.cloned.1.call-start = ((), (), s32[]{:S(2)}) async-start(), calls=%async_computation.25 | async-start | bytes 9437184 | tf_op jit(solution)/shard_map/reduce_scatter | solution.py:185
  433.9 257.5 %reduce-scatter.38.cloned.1.call-start = ((), (), s32[]{:S(2)}) async-start(), calls=%async_computation.26 | async-start | bytes 9437184 | tf_op jit(solution)/shard_map/reduce_scatter | solution.py:188
  451.1 272.0 %reduce-scatter.42.cloned.1.call-start = ((), (), s32[]{:S(2)}) async-start(), calls=%async_computation.28 | async-start | bytes 36864
  500.8 253.8 %reduce-scatter.40.cloned.1.call-start = ((), (), s32[]{:S(2)}) async-start(), calls=%async_computation.27 | async-start | bytes 36864
  514.0 276.8 %reduce-scatter.34.cloned.1.call-start = ((), (), s32[]{:S(2)}) async-start(), calls=%async_computation.24 | async-start | bytes 2359296 | tf_op jit(solution)/shard_map/reduce_scatter | solution.py:182
  521.3 306.4 %reduce-scatter.32.cloned.1.call-start = ((), (), s32[]{:S(2)}) async-start(), calls=%async_computation.23 | async-start | bytes 2359296 | tf_op jit(solution)/shard_map/reduce_scatter | solution.py:173
  528.2 336.4 %reduce-scatter.28.cloned.1.call-start = ((), (), s32[]{:S(2)}) async-start(), calls=%async_computation.21 | async-start | bytes 2359296 | tf_op jit(solution)/shard_map/reduce_scatter | solution.py:167
  535.0 366.4 %reduce-scatter.30.cloned.1.call-start = ((), (), s32[]{:S(2)}) async-start(), calls=%async_computation.22 | async-start | bytes 2359296 | tf_op jit(solution)/shard_map/reduce_scatter | solution.py:170
  549.2 415.0 %reduce-scatter.26.cloned.1.call-start = ((), (), s32[]{:S(2)}) async-start(), calls=%async_computation.20 | async-start | bytes 6553600 | tf_op jit(solution)/shard_map/reduce_scatter | solution.py:160
  573.2 456.0 %reduce-scatter.22.cloned.1.call-start = ((), (), s32[]{:S(2)}) async-start(), calls=%async_computation.16 | async-start | bytes 6553600 | tf_op jit(solution)/shard_map/reduce_scatter | solution.py:91
  603.9 360.4 %copy-start.3 = (bf16[2,160,2048]{2,1,0:T(8,128)(2,1)S(1)}, bf16[2,160,2048]{2,1,0:T(8,128)(2,1)}, u32[]{:S(2)}) copy-start(bf16[2,160,2048]{2,1,0:T(8,128)(2,1)} %param.18) | copy-start | bytes 3932164
  603.9 360.4 %copy-start.27 = (f32[2048]{0:T(1024)S(1)}, f32[2048]{0:T(1024)}, u32[]{:S(2)}) copy-start(f32[2048]{0:T(1024)} %param.31) | copy-start | bytes 24580
  603.9 360.4 %copy-start.31 = (f32[2,160]{1,0:T(2,128)S(1)}, f32[2,160]{1,0:T(2,128)}, u32[]{:S(2)}) copy-start(f32[2,160]{1,0:T(2,128)} %copy-done.30) | copy-start | bytes 3844
  792.6 173.9 %copy-start.25 = (f32[2,160]{1,0:T(2,128)S(1)}, f32[2,160]{1,0:T(2,128)}, u32[]{:S(2)}) copy-start(f32[2,160]{1,0:T(2,128)} %copy-done.24) | copy-start | bytes 3844
  792.6 173.9 %copy-start.29 = (f32[2,160]{1,0:T(2,128)S(1)}, f32[2,160]{1,0:T(2,128)}, u32[]{:S(2)}) copy-start(f32[2,160]{1,0:T(2,128)} %copy-done.28) | copy-start | bytes 3844
  (48 other events, 1852.1 us)
Sparse Core Ops, SparseCore 0:
  13.8 64.0 all-gather.4
  115.0 61.3 reduce-scatter.19
  181.1 61.3 all-gather.6
  244.2 61.2 all-gather.8
  347.2 61.3 reduce-scatter.23
  416.4 61.2 all-gather.10
  480.6 30.4 reduce-scatter.43
  513.4 87.6 reduce-scatter.35
  603.4 87.9 reduce-scatter.37
  694.1 28.9 reduce-scatter.41
  725.9 28.5 reduce-scatter.39
  756.7 34.0 reduce-scatter.33
  793.1 34.5 reduce-scatter.31
  829.9 34.6 reduce-scatter.27
  866.7 34.6 reduce-scatter.29
  904.3 59.9 reduce-scatter.25
  967.1 62.1 reduce-scatter.21
where the time goes:
time: 1050 us; the launch traced here: 1040 us
  waiting for transfers between devices  656 us (62%)
  matrix products  227 us (22%)
  other arithmetic  81.9 us (8%)
  blocking collectives  40.7 us (4%)
  local copies, waits for them, and re-layouts  18.7 us (2%)
  between operations  15 us (1%)
    reduce_scatter x1, waiting for transfers between devices, body(): lax.psum_scatter(grad_w_down.astype(jnp.bfloat16), 'dp', scatter_dimensio...  87.5 us
    all_gather x1, waiting for transfers between devices, body(): full_one = lax.all_gather(normed_one, 'mp', axis=1, tiled=True)  62.6 us
    reduce_scatter x1, waiting for transfers between devices, body(): lax.psum_scatter(attn_terms.astype(jnp.bfloat16), 'mp', scatter_dimension...  61.4 us
    reduce_scatter x1, waiting for transfers between devices, body(): lax.psum_scatter(back_terms.astype(jnp.bfloat16), 'mp', scatter_dimension...  61.2 us
    reduce_scatter x1, waiting for transfers between devices, body(): lax.psum_scatter(back_one.astype(jnp.bfloat16), 'mp', scatter_dimension=1...  61 us
    all_gather x1, waiting for transfers between devices, body(): full_two = lax.all_gather(normed_two, 'mp', axis=1, tiled=True)  60.4 us
    unnamed x20, waiting for transfers between devices  59.9 us
    unnamed x1, blocking collectives  40.7 us
  transfers between devices with their start and end apart: 17, of which 16 were waited for; matrix products, arithmetic and copies ran while one was open for 21% of the time, Pallas kernels for 0%

commit v1 on v0

--- a/solution.py
+++ b/solution.py
@@ -109,7 +109,15 @@
     grad_mid_norm, grad_gain_two, grad_shift_two = second_back(back_rows)
     grad_middle = grad_out + grad_mid_norm
     grad_b_out = jnp.sum(grad_middle, axis=(0, 1))
-    middle_full = lax.all_gather(grad_middle.astype(bf16), "mp", axis=1, tiled=True)
+    x = grad_middle.astype(bf16)
+    ways, here, step = (lax.axis_size("mp"), lax.axis_index("mp"), x.shape[1])
+    line, have = (x, 1)
+    while have < ways:
+        line = jnp.concatenate(
+            [line, lax.ppermute(line, "mp", [(d, (d - have) % ways) for d in range(ways)])], axis=1
+        )
+        have = 2 * have
+    middle_full = jnp.roll(line, here * step, axis=1)
     grad_w_out = jnp.einsum("ise,isd->ed", mixed, middle_full, preferred_element_type=f32)
     grad_mixed = (
         jnp.einsum("isd,ed->ise", middle_full, w_out, preferred_element_type=f32)

time: 1050 us -> 1070 us (1.019)
  waiting for transfers between devices: 656 us -> 668 us
    ppermute x0 -> x2, waiting for transfers between devices: none -> 83.4 us  [body(): lax.ppermute(line, 'mp', [(d, (d - have) % ways) for d in range(ways)])]
    unnamed x20 -> x19, waiting for transfers between devices: 59.9 us -> 0.79 us
    all_gather x1 -> x0, waiting for transfers between devices: 26.6 us -> none  [body(): lax.all_gather(grad_middle.astype(bf16), 'mp', axis=1, tiled=True)]
    reduce_scatter x1, waiting for transfers between devices: 9.5 us -> 25.2 us  [body(): lax.psum_scatter(grad_w_up.astype(jnp.bfloat16), 'dp', scatter_dimension=...]
    unnamed x122 -> x138, local copies, waits for them, and re-layouts: 18.7 us -> 25.1 us
  transfers between devices with their start and end apart: 17 -> 18, of which waited for: 16 -> 15; matrix products, arithmetic and copies ran while one was open for 21% -> 21% of each run, Pallas kernels for 0% -> 0%
where the time goes in v1:
time: 1070 us; the launch traced here: 1060 us
  waiting for transfers between devices  668 us (62%)
  matrix products  220 us (21%)
  other arithmetic  83.7 us (8%)
  blocking collectives  40.7 us (4%)
  local copies, waits for them, and re-layouts  28.8 us (3%)
  between operations  15 us (1%)
    reduce_scatter x1, waiting for transfers between devices, body(): lax.psum_scatter(grad_w_down.astype(jnp.bfloat16), 'dp', scatter_dimensio...  87.4 us
    ppermute x2, waiting for transfers between devices, body(): lax.ppermute(line, 'mp', [(d, (d - have) % ways) for d in range(ways)])  83.4 us
    all_gather x1, waiting for transfers between devices, body(): full_one = lax.all_gather(normed_one, 'mp', axis=1, tiled=True)  62.6 us
    reduce_scatter x1, waiting for transfers between devices, body(): lax.psum_scatter(attn_terms.astype(jnp.bfloat16), 'mp', scatter_dimension...  61.4 us
    reduce_scatter x1, waiting for transfers between devices, body(): lax.psum_scatter(back_terms.astype(jnp.bfloat16), 'mp', scatter_dimension...  61.2 us
    reduce_scatter x1, waiting for transfers between devices, body(): lax.psum_scatter(back_one.astype(jnp.bfloat16), 'mp', scatter_dimension=1...  61.1 us
    all_gather x1, waiting for transfers between devices, body(): full_two = lax.all_gather(normed_two, 'mp', axis=1, tiled=True)  60.4 us
    unnamed x1, blocking collectives  40.7 us
  transfers between devices with their start and end apart: 18, of which 15 were waited for; matrix products, arithmetic and copies ran while one was open for 21% of the time, Pallas kernels for 0%

profile of v1, /device:TPU:0, one launch (start us, length us, event | category | flops | bytes accessed | tf_op | source)
XLA Modules:
  0.0 1062.1 jit_solution(9291037879762952427)
XLA Ops:
  15.3 62.6 %all-gather.4.cloned.1.call-done = bf16[2,640,2048]{2,1,0:T(8,128)(2,1)} async-done(((bf16[2,160,2048]{2,1,0:T(8,128)(2,1)}), bf16[2,640,2048]{2,1,0:T(8,128)(2,1)}) %all-gather.4.cloned.1.call-update) | async-done | bytes 5242896 | tf_op jit(solution)/shard_map/all_gather | solution.py:54
  89.4 11.4 %fusion.102 = (f32[2,4,640]{2,1,0:T(4,128)S(1)}, f32[2,4,640,640]{2,3,1,0:T(8,128)}) fusion(pred[2,640,640]{1,2,0:T(8,128)(4,1)} %broadcast_and_fusion, bf16[2,640,4,128]{1,3,2,0:T(8,128)(2,1)} %bitcast.133, bf16[2,640,4,128]{1,3,2,0:T(8,128)(2,1)} %bitcast.127), kind=kOutput, calls=%fused_computation.146 | convolution fusion | flops 851968640 | bytes 16568320 | tf_op jit(solution)/shard_map/sub | solution.py:71
  115.0 61.4 %reduce-scatter.20.cloned.1.call-done = bf16[2,160,2048]{2,1,0:T(8,128)(2,1)} async-done(((bf16[2,640,2048]{2,1,0:T(8,128)(2,1)}), bf16[2,160,2048]{2,1,0:T(8,128)(2,1)}) %reduce-scatter.20.cloned.1.call-update) | async-done | bytes 1310736 | tf_op jit(solution)/shard_map/reduce_scatter | solution.py:80
  182.1 60.4 %all-gather.6.cloned.1.call-done = bf16[2,640,2048]{2,1,0:T(8,128)(2,1)} async-done(((bf16[2,160,2048]{2,1,0:T(8,128)(2,1)}), bf16[2,640,2048]{2,1,0:T(8,128)(2,1)}) %all-gather.6.cloned.1.call-update) | async-done | bytes 5242896 | tf_op jit(solution)/shard_map/all_gather | solution.py:85
  242.5 20.1 %fusion.54 = (u8[640,2048]{1,0:T(8,128)(4,1)}, u8[640,2048]{1,0:T(8,128)(4,1)}, f32[2,640,2048]{2,1,0:T(8,128)S(1)}) fusion(f32[2048]{0:T(1024)S(1)} %bitcast.140, bf16[2,640,2048]{2,1,0:T(8,128)(2,1)} %all-gather.6.cloned.1.call-done, bf16[2048,2048]{1,0:T(8,128)(2,1)} %param.27), kind=kOutput, calls=%fused_computation.96 | convolution fusion | flops 10771496960 | bytes 26746880 | tf_op jit(solution)/shard_map/isd,df->isf/dot_general | solution.py:86
  266.5 26.8 %multiply_convert_fusion.1 = (bf16[2,640,2048]{2,1,0:T(8,128)(2,1)}, f32[2,640,2048]{2,1,0:T(8,128)}) fusion(f32[2,640,2048]{2,1,0:T(8,128)S(1)} %get-tuple-element.43, f32[2048]{0:T(1024)S(1)} %bitcast.141, u8[640,2048]{1,0:T(8,128)(4,1)} %get-tuple-element.18, u8[640,2048]{1,0:T(8,128)(4,1)} %get-tuple-element.17), kind=kLoop, calls=%fused_computation.16 | loop fusion | flops 186122240 | bytes 28844032 | tf_op jit(solution)/shard_map/convert_element_type | solution.py:89
  293.2 12.3 %all-gather.8.cloned.1.call-done = bf16[2,640,2048]{2,1,0:T(8,128)(2,1)} async-done(((bf16[2,160,2048]{2,1,0:T(8,128)(2,1)}), bf16[2,640,2048]{2,1,0:T(8,128)(2,1)}) %all-gather.8.cloned.1.call-update) | async-done | bytes 5242896 | tf_op jit(solution)/shard_map/all_gather | solution.py:96
  305.6 25.0 %fusion.103 = (bf16[2048]{0:T(1024)(128)(2,1)S(1)}, bf16[2,640,2048]{2,1,0:T(8,128)(2,1)}) fusion(f32[2,640,2048]{2,1,0:T(8,128)} %get-tuple-element.38, bf16[2,640,2048]{2,1,0:T(8,128)(2,1)} %all-gather.8.cloned.1.call-done, bf16[2048,2048]{1,0:T(8,128)(2,1)} %param.29, f32[2,640,2048]{2,1,0:T(8,128)} %copy-done.15, f32[2048]{0:T(1024)S(1)} %bitcast.142), kind=kOutput, calls=%fused_computation.147 | convolution fusion | flops 10779359232 | bytes 39858176 | tf_op jit(solution)/shard_map/isd,fd->isf/dot_general | solution.py:99
  330.5 16.6 %fusion.25 = bf16[2,640,2048]{2,1,0:T(8,128)(2,1)} fusion(bf16[2,640,2048]{2,1,0:T(8,128)(2,1)} %get-tuple-element.51, bf16[2048,2048]{1,0:T(8,128)(2,1)} %param.27), kind=kOutput, calls=%fused_computation.50 | convolution fusion | flops 10740039680 | bytes 18874368 | tf_op jit(solution)/shard_map/isf,df->isd/dot_general | solution.py:104
  347.4 61.2 %reduce-scatter.24.cloned.1.call-done = bf16[2,160,2048]{2,1,0:T(8,128)(2,1)} async-done(((bf16[2,640,2048]{2,1,0:T(8,128)(2,1)}), bf16[2,160,2048]{2,1,0:T(8,128)(2,1)}) %reduce-scatter.24.cloned.1.call-update) | async-done | bytes 1310736 | tf_op jit(solution)/shard_map/reduce_scatter | solution.py:105
  417.3 28.9 %collective-permute-done = bf16[2,160,2048]{2,1,0:T(8,128)(2,1)S(1)} collective-permute-done((bf16[2,160,2048]{2,1,0:T(8,128)(2,1)S(1)}, bf16[2,160,2048]{2,1,0:T(8,128)(2,1)S(1)}, u32[]{:S(2)}, u32[]{:S(2)}) %collective-permute-start) | collective-permute-done | bytes 1310752 | tf_op jit(solution)/shard_map/ppermute | solution.py:117
  451.4 54.5 %collective-permute-done.1 = bf16[2,320,2048]{2,1,0:T(8,128)(2,1)} collective-permute-done((bf16[2,320,2048]{2,1,0:T(8,128)(2,1)}, bf16[2,320,2048]{2,1,0:T(8,128)(2,1)}, u32[]{:S(2)}, u32[]{:S(2)}) %collective-permute-start.1) | collective-permute-done | bytes 2621472 | tf_op jit(solution)/shard_map/ppermute | solution.py:117
  544.4 16.7 %bitcast_convert_fusion.1 = bf16[2048,2048]{1,0:T(8,128)(2,1)} fusion(bf16[2,640,2048]{2,1,0:T(8,128)(2,1)} %all-gather.6.cloned.1.call-done, bf16[2,640,2048]{2,1,0:T(8,128)(2,1)} %get-tuple-element.51), kind=kOutput, calls=%fused_computation.2 | convolution fusion | flops 10741612544 | bytes 18874368 | tf_op jit(solution)/shard_map/isd,isf->df/dot_general | solution.py:102
  561.3 16.7 %bitcast_convert_fusion = bf16[2048,2048]{1,0:T(8,128)(2,1)} fusion(bf16[2,640,2048]{2,1,0:T(8,128)(2,1)} %get-tuple-element.37, bf16[2,640,2048]{2,1,0:T(8,128)(2,1)} %all-gather.8.cloned.1.call-done), kind=kOutput, calls=%fused_computation.1 | convolution fusion | flops 10741612544 | bytes 18874368 | tf_op jit(solution)/shard_map/isf,isd->fd/dot_general | solution.py:97
  638.1 16.6 %fusion.28 = bf16[2,640,2048]{2,1,0:T(8,128)(2,1)} fusion(bf16[2,640,2048]{2,1,0:T(8,128)(2,1)} %get-tuple-element.37, bf16[2048,2048]{1,0:T(8,128)(2,1)} %param.29), kind=kOutput, calls=%fused_computation.51 | convolution fusion | flops 10740039680 | bytes 18874368 | tf_op jit(solution)/shard_map/isf,fd->isd/dot_general | solution.py:90
  658.9 25.2 %reduce-scatter.36.cloned.1.call-done = bf16[256,2048]{1,0:T(8,128)(2,1)} async-done(((bf16[2048,2048]{1,0:T(8,128)(2,1)}), bf16[256,2048]{1,0:T(8,128)(2,1)}) %reduce-scatter.36.cloned.1.call-update) | async-done | bytes 1048592 | tf_op jit(solution)/shard_map/reduce_scatter | solution.py:193
  686.9 87.4 %reduce-scatter.38.cloned.1.call-done = bf16[2048,256]{1,0:T(8,128)(2,1)} async-done(((bf16[2048,2048]{1,0:T(8,128)(2,1)}), bf16[2048,256]{1,0:T(8,128)(2,1)}) %reduce-scatter.38.cloned.1.call-update) | async-done | bytes 1048592 | tf_op jit(solution)/shard_map/reduce_scatter | solution.py:196
  776.9 34.1 %reduce-scatter.34.cloned.1.call-done = bf16[512,256]{1,0:T(8,128)(2,1)} async-done(((bf16[512,2048]{1,0:T(8,128)(2,1)}), bf16[512,256]{1,0:T(8,128)(2,1)}) %reduce-scatter.34.cloned.1.call-update) | async-done | bytes 262160 | tf_op jit(solution)/shard_map/reduce_scatter | solution.py:190
  812.9 35.0 %reduce-scatter.32.cloned.1.call-done = bf16[256,512]{1,0:T(8,128)(2,1)} async-done(((bf16[2048,512]{1,0:T(8,128)(2,1)}), bf16[256,512]{1,0:T(8,128)(2,1)}) %reduce-scatter.32.cloned.1.call-update) | async-done | bytes 262160 | tf_op jit(solution)/shard_map/reduce_scatter | solution.py:181
  849.7 35.1 %reduce-scatter.28.cloned.1.call-done = bf16[256,512]{1,0:T(8,128)(2,1)} async-done(((bf16[2048,512]{1,0:T(8,128)(2,1)}), bf16[256,512]{1,0:T(8,128)(2,1)}) %reduce-scatter.28.cloned.1.call-update) | async-done | bytes 262160 | tf_op jit(solution)/shard_map/reduce_scatter | solution.py:175
  886.6 34.8 %reduce-scatter.30.cloned.1.call-done = bf16[256,512]{1,0:T(8,128)(2,1)} async-done(((bf16[2048,512]{1,0:T(8,128)(2,1)}), bf16[256,512]{1,0:T(8,128)(2,1)}) %reduce-scatter.30.cloned.1.call-update) | async-done | bytes 262160 | tf_op jit(solution)/shard_map/reduce_scatter | solution.py:178
  923.3 61.1 %reduce-scatter.26.cloned.1.call-done = bf16[2,160,2048]{2,1,0:T(8,128)(2,1)} async-done(((bf16[2,640,2048]{2,1,0:T(8,128)(2,1)}), bf16[2,160,2048]{2,1,0:T(8,128)(2,1)}) %reduce-scatter.26.cloned.1.call-update) | async-done | bytes 1310736 | tf_op jit(solution)/shard_map/reduce_scatter | solution.py:168
  991.8 40.7 %all-reduce.6 = (f32[2048]{0:T(1024)S(1)}, f32[2048]{0:T(1024)S(1)}, f32[2048]{0:T(1024)S(1)}, f32[2048]{0:T(1024)S(1)}, f32[2048]{0:T(1024)S(1)}, /*index=5*/f32[2048]{0:T(1024)S(1)}) all-reduce(f32[2048]{0:T(1024)S(1)} %get-tuple-element.20, f32[2048]{0:T(1024)S(1)} %get-tuple-element.23, ...), channel_id=12, replica_groups=mesh['dp'=8,'mp'=4] {'dp','mp'}, use_global_device_ids=true, to_apply=%region_24.25.clone | all-reduce | flops 12288 | bytes 98304
  1036.0 13.4 %reduce-scatter.22.cloned.1.call-done = bf16[2,160,2048]{2,1,0:T(8,128)(2,1)} async-done(((bf16[2,640,2048]{2,1,0:T(8,128)(2,1)}), bf16[2,160,2048]{2,1,0:T(8,128)(2,1)}) %reduce-scatter.22.cloned.1.call-update) | async-done | bytes 1310736 | tf_op jit(solution)/shard_map/reduce_scatter | solution.py:91
  (228 shorter events, 189.2 us)
Async XLA Ops:
  7.2 70.6 %all-gather.4.cloned.1.call-start = ((), (), s32[]{:S(2)}) async-start(), calls=%async_computation.13 | async-start | bytes 6553600 | tf_op jit(solution)/shard_map/all_gather | solution.py:54
  13.7 162.8 %reduce-scatter.20.cloned.1.call-start = ((), (), s32[]{:S(2)}) async-start(), calls=%async_computation.14 | async-start | bytes 6553600 | tf_op jit(solution)/shard_map/reduce_scatter | solution.py:80
  115.0 127.5 %all-gather.6.cloned.1.call-start = ((), (), s32[]{:S(2)}) async-start(), calls=%async_computation.15 | async-start | bytes 6553600 | tf_op jit(solution)/shard_map/all_gather | solution.py:85
  178.4 235.0 %copy-start.26 = (f32[2,160]{1,0:T(2,128)}, f32[2,160]{1,0:T(2,128)S(1)}, u32[]{:S(2)}) copy-start(f32[2,160]{1,0:T(2,128)S(1)} %broadcast_multiply_fusion) | copy-start | bytes 3844
  179.1 234.3 %copy-start.32 = (f32[2,160]{1,0:T(2,128)}, f32[2,160]{1,0:T(2,128)S(1)}, u32[]{:S(2)}) copy-start(f32[2,160]{1,0:T(2,128)S(1)} %fusion.93) | copy-start | bytes 3844
  181.1 124.5 %all-gather.8.cloned.1.call-start = ((), (), s32[]{:S(2)}) async-start(), calls=%async_computation.17 | async-start | bytes 6553600 | tf_op jit(solution)/shard_map/all_gather | solution.py:96
  181.7 227.0 %reduce-scatter.24.cloned.1.call-start = ((), (), s32[]{:S(2)}) async-start(), calls=%async_computation.18 | async-start | bytes 6553600 | tf_op jit(solution)/shard_map/reduce_scatter | solution.py:105
  347.2 307.7 %reduce-scatter.44.cloned.1.call-start = ((), (), s32[]{:S(2)}) async-start(), calls=%async_computation.28 | async-start | bytes 36864
  415.9 30.4 %collective-permute-start = (bf16[2,160,2048]{2,1,0:T(8,128)(2,1)S(1)}, bf16[2,160,2048]{2,1,0:T(8,128)(2,1)S(1)}, u32[]{:S(2)}, u32[]{:S(2)}) collective-permute-start(bf16[2,160,2048]{2,1,0:T(8,128)(2,1)S(1)} %get-tuple-element.36), channel_id=1, source_target_pairs={{0,3},{1,0},{2,1},{3,2},{4,7},{5,4},{6,5},{7,6},{8,11},{9,8},{10,9... | collective-permute-start | bytes 3932168 | tf_op jit(solution)/shard_map/ppermute | solution.py:117
  448.0 57.9 %collective-permute-start.1 = (bf16[2,320,2048]{2,1,0:T(8,128)(2,1)}, bf16[2,320,2048]{2,1,0:T(8,128)(2,1)}, u32[]{:S(2)}, u32[]{:S(2)}) collective-permute-start(bf16[2,320,2048]{2,1,0:T(8,128)(2,1)} %pad_maximum_fusion), channel_id=1, source_target_pairs={{0,2},{1,3},{2,0},{3,1},{4,6},{5,7},{6,4},{7,5},{8,10},{9,11},{10,... | collective-permute-start | bytes 7864328 | tf_op jit(solution)/shard_map/ppermute | solution.py:117
  450.2 206.0 %reduce-scatter.42.cloned.1.call-start = ((), (), s32[]{:S(2)}) async-start(), calls=%async_computation.27 | async-start | bytes 36864
  530.9 126.6 %reduce-scatter.40.cloned.1.call-start = ((), (), s32[]{:S(2)}) async-start(), calls=%async_computation.26 | async-start | bytes 36864
  544.4 139.7 %reduce-scatter.36.cloned.1.call-start = ((), (), s32[]{:S(2)}) async-start(), calls=%async_computation.24 | async-start | bytes 9437184 | tf_op jit(solution)/shard_map/reduce_scatter | solution.py:193
  561.1 213.1 %reduce-scatter.38.cloned.1.call-start = ((), (), s32[]{:S(2)}) async-start(), calls=%async_computation.25 | async-start | bytes 9437184 | tf_op jit(solution)/shard_map/reduce_scatter | solution.py:196
  578.0 233.0 %reduce-scatter.34.cloned.1.call-start = ((), (), s32[]{:S(2)}) async-start(), calls=%async_computation.23 | async-start | bytes 2359296 | tf_op jit(solution)/shard_map/reduce_scatter | solution.py:190
  585.3 262.6 %reduce-scatter.32.cloned.1.call-start = ((), (), s32[]{:S(2)}) async-start(), calls=%async_computation.22 | async-start | bytes 2359296 | tf_op jit(solution)/shard_map/reduce_scatter | solution.py:181
  592.2 292.7 %reduce-scatter.28.cloned.1.call-start = ((), (), s32[]{:S(2)}) async-start(), calls=%async_computation.20 | async-start | bytes 2359296 | tf_op jit(solution)/shard_map/reduce_scatter | solution.py:175
  599.0 322.4 %reduce-scatter.30.cloned.1.call-start = ((), (), s32[]{:S(2)}) async-start(), calls=%async_computation.21 | async-start | bytes 2359296 | tf_op jit(solution)/shard_map/reduce_scatter | solution.py:178
  613.6 370.7 %reduce-scatter.26.cloned.1.call-start = ((), (), s32[]{:S(2)}) async-start(), calls=%async_computation.19 | async-start | bytes 6553600 | tf_op jit(solution)/shard_map/reduce_scatter | solution.py:168
  637.8 411.5 %reduce-scatter.22.cloned.1.call-start = ((), (), s32[]{:S(2)}) async-start(), calls=%async_computation.16 | async-start | bytes 6553600 | tf_op jit(solution)/shard_map/reduce_scatter | solution.py:91
  686.9 297.5 %copy-start.3 = (bf16[2,160,2048]{2,1,0:T(8,128)(2,1)S(1)}, bf16[2,160,2048]{2,1,0:T(8,128)(2,1)}, u32[]{:S(2)}) copy-start(bf16[2,160,2048]{2,1,0:T(8,128)(2,1)} %param.18) | copy-start | bytes 3932164
  686.9 297.5 %copy-start.29 = (f32[2048]{0:T(1024)S(1)}, f32[2048]{0:T(1024)}, u32[]{:S(2)}) copy-start(f32[2048]{0:T(1024)} %param.31) | copy-start | bytes 24580
  686.9 297.5 %copy-start.31 = (f32[2,160]{1,0:T(2,128)S(1)}, f32[2,160]{1,0:T(2,128)}, u32[]{:S(2)}) copy-start(f32[2,160]{1,0:T(2,128)} %copy-done.30) | copy-start | bytes 3844
  812.8 173.7 %copy-start.27 = (f32[2,160]{1,0:T(2,128)S(1)}, f32[2,160]{1,0:T(2,128)}, u32[]{:S(2)}) copy-start(f32[2,160]{1,0:T(2,128)} %copy-done.26) | copy-start | bytes 3844
  (55 other events, 2145.7 us)
Sparse Core Ops, SparseCore 0:
  13.8 64.0 all-gather.3
  115.1 61.3 reduce-scatter.19
  181.2 61.2 all-gather.5
  244.2 61.2 all-gather.7
  347.3 61.3 reduce-scatter.23
  450.3 31.4 reduce-scatter.43
  531.0 31.3 reduce-scatter.41
  565.2 28.6 reduce-scatter.39
  596.2 87.7 reduce-scatter.35
  686.2 87.9 reduce-scatter.37
  776.5 34.4 reduce-scatter.33
  813.2 34.6 reduce-scatter.31
  850.2 34.5 reduce-scatter.27
  887.0 34.4 reduce-scatter.29
  924.3 60.0 reduce-scatter.25
  987.2 62.1 reduce-scatter.21
